TPU v7x, 128 devices: a whole 4x4x4 slice. The times are simulated.
128 devices in a mesh: grp: 8 (over z, core), dev: 16 (over y, x).
Axes of the slice: x: 4, y: 4, z: 4, core: 2. Of those that a mesh axis runs over, the one named last changes fastest.
Arguments:
- positions: float32 [3, 131072], P(None, ('grp', 'dev')), may hold values from -3 to 3
- velocities: float32 [3, 131072], P(None, ('grp', 'dev')), may hold values from -5 to 5
- accelerations: float32 [3, 131072], P(None, ('grp', 'dev')), may hold values from -3 to 3
- jerks: float32 [3, 131072], P(None, ('grp', 'dev')), may hold values from -3 to 3
- levels: int32 [131072], P(('grp', 'dev')), may hold values from 0 to 5
- counts: int32 [2, 128], replicated, may hold values from 1 to 256, 16384 in all within a row
- active_rows: int32 [2, 32768], P(None, ('grp', 'dev')), may hold values from 0 to 1023, as said below
Outputs:
- new_positions: float32 [3, 131072], P(None, ('grp', 'dev'))
- new_velocities: float32 [3, 131072], P(None, ('grp', 'dev'))
- new_accelerations: float32 [3, 131072], P(None, ('grp', 'dev'))
- new_jerks: float32 [3, 131072], P(None, ('grp', 'dev'))
Inputs may be any that keep to these rules, and one draw needn't show every extreme that they name: In each step the 128 counts sum to exactly 16384 and the largest of them is exactly 256. `active_rows`: for each step and device, the 256 entries of the device's slots are distinct indices of that device's own stars; only the first counts of them are live.
All inputs are finite; a program needn't handle non-finite values.
Results may differ from a plain program's by a relative error of at most 0.00022.
Values sent between devices are 32-bit elements; how exact they have to be, the bound alone decides.
No kernel may reach another device: no remote copies, remote signals or barrier semaphores. Data moves between devices by JAX's collectives and lax.ppermute only.
A program may use at most 128 MiB of HBM per device.

v0:
```python
import math

import jax
import jax.numpy as jnp
from jax import lax
from jax.sharding import PartitionSpec as P

tick_length = 1.0 / 128.0


def pair_block(targets, src_pos, src_vel, mass, soft_sq):
    gap_x = src_pos[0][None, :] - targets[0][:, None]
    gap_y = src_pos[1][None, :] - targets[1][:, None]
    gap_z = src_pos[2][None, :] - targets[2][:, None]
    drift_x = src_vel[0][None, :] - targets[3][:, None]
    drift_y = src_vel[1][None, :] - targets[4][:, None]
    drift_z = src_vel[2][None, :] - targets[5][:, None]
    squared = gap_x * gap_x + gap_y * gap_y + gap_z * gap_z + soft_sq
    inverse = lax.rsqrt(squared)
    weight = mass * inverse * inverse * inverse
    along = 3.0 * (gap_x * drift_x + gap_y * drift_y + gap_z * drift_z) * inverse * inverse
    return jnp.stack(
        [
            jnp.sum(weight * gap_x, axis=1),
            jnp.sum(weight * gap_y, axis=1),
            jnp.sum(weight * gap_z, axis=1),
            jnp.sum(weight * (drift_x - along * gap_x), axis=1),
            jnp.sum(weight * (drift_y - along * gap_y), axis=1),
            jnp.sum(weight * (drift_z - along * gap_z), axis=1),
        ]
    )


def block_terms(packed, src_pos, src_vel, mass, soft_sq):
    width, total = packed.shape
    block = math.gcd(total, 2048)
    grouped = packed.reshape(width, total // block, block).transpose(1, 0, 2)
    result = lax.map(lambda targets: pair_block(targets, src_pos, src_vel, mass, soft_sq), grouped)
    return result.transpose(1, 0, 2).reshape(width, total)


def predict(positions, velocities, accelerations, jerks, elapsed):
    span = elapsed[None, :]
    pred_pos = (
        positions
        + span * velocities
        + 0.5 * span * span * accelerations
        + span * span * span / 6.0 * jerks
    )
    pred_vel = velocities + span * accelerations + 0.5 * span * span * jerks
    return (pred_pos, pred_vel)


def correct(old_pos, old_vel, old_acc, old_jerk, force, jerk_new, span):
    span = span[None, :]
    new_vel = old_vel + 0.5 * span * (old_acc + force) + span * span / 12.0 * (old_jerk - jerk_new)
    new_pos = old_pos + 0.5 * span * (old_vel + new_vel) + span * span / 12.0 * (old_acc - force)
    return (new_pos, new_vel)


def shards(positions, velocities, accelerations, jerks, levels, counts, active_rows):
    devices_all = lax.axis_size("grp") * lax.axis_size("dev")
    my_rank = lax.axis_index("grp") * lax.axis_size("dev") + lax.axis_index("dev")
    star_dev = positions.shape[1]
    slot_cap = active_rows.shape[1]
    stars_all = star_dev * devices_all
    mass = 1.0 / stars_all
    soft_sq = 0.0004 * (131072.0 / stars_all) ** (2.0 / 3.0)
    last_time = -(jnp.left_shift(jnp.int32(1), levels) - 1).astype(jnp.float32) * tick_length
    for step in range(active_rows.shape[0]):
        now = (step + 1) * tick_length
        pred_pos, pred_vel = predict(positions, velocities, accelerations, jerks, now - last_time)
        rows = active_rows[step]
        targets = jnp.concatenate([pred_pos[:, rows], pred_vel[:, rows]], axis=0)
        step_counts = counts[step]
        own_count = step_counts[my_rank]
        gathered = lax.all_gather(targets[None], ("grp", "dev"), axis=0, tiled=True)
        flat = gathered.transpose(1, 0, 2).reshape(6, devices_all * slot_cap)
        terms = block_terms(flat, pred_pos, pred_vel, mass, soft_sq)
        totals = lax.psum(terms, ("grp", "dev"))
        own = lax.dynamic_slice_in_dim(totals, my_rank * slot_cap, slot_cap, 1)
        span = now - last_time[rows]
        new_pos, new_vel = correct(
            positions[:, rows],
            velocities[:, rows],
            accelerations[:, rows],
            jerks[:, rows],
            own[:3],
            own[3:],
            span,
        )
        live = jnp.arange(slot_cap, dtype=jnp.int32) < own_count
        target = jnp.where(live, rows, star_dev)
        positions = positions.at[:, target].set(new_pos, mode="drop")
        velocities = velocities.at[:, target].set(new_vel, mode="drop")
        accelerations = accelerations.at[:, target].set(own[:3], mode="drop")
        jerks = jerks.at[:, target].set(own[3:], mode="drop")
        last_time = last_time.at[target].set(now, mode="drop")
    return (positions, velocities, accelerations, jerks)


def solution(mesh):
    placed = (
        P(None, ("grp", "dev")),
        P(None, ("grp", "dev")),
        P(None, ("grp", "dev")),
        P(None, ("grp", "dev")),
        P(("grp", "dev")),
        P(),
        P(None, ("grp", "dev")),
    )
    return jax.shard_map(
        shards,
        mesh=mesh,
        in_specs=placed,
        out_specs=(
            P(None, ("grp", "dev")),
            P(None, ("grp", "dev")),
            P(None, ("grp", "dev")),
            P(None, ("grp", "dev")),
        ),
        check_vma=False,
    )
```

profile of v0, /device:TPU:1, one launch (start us, length us, event | category | flops | bytes accessed | tf_op | source)
XLA Modules:
  0.0 1007.8 jit_solution(7098034643428185469)
XLA Ops:
  8.6 2.1 compare_select_fusion
  14.2 63.9 %all-gather.2 = f32[128,6,256]{2,1,0:T(8,128)S(1)} all-gather(f32[1,6,256]{2,1,0:T(8,128)S(1)} %maximum_bitcast_fusion), channel_id=2, replica_groups=mesh['grp'=8,'dev'=16] {'grp','dev'}, dimensions={0}, use_global_device_ids=true | all-gather | bytes 792576 | tf_op jit(solution)/shard_map/all_gather | solution.py:77
  78.2 263.2 %while.20 = (s32[]{:T(128)}, f32[16,6,2048]{2,1,0:T(8,128)S(1)}, f32[3,1024]{1,0:T(4,128)S(1)}, f32[16,6,2048]{2,1,0:T(8,128)S(1)}, f32[3,1024]{1,0:T(4,128)S(1)...) while((s32[]{:T(128)}, f32[16,6,2048]{2,1,0:T(8,128)S(1)}, ...), condition=%wide.region_7.8_spmd, body=%wide.region_0.7_spmd.sunk | while | flops 85970952 | bytes 499917 | solution.py:38
  78.3 16.2 %fusion.64 = (f32[2048]{0:T(1024)S(1)}, f32[2048]{0:T(1024)S(1)}, f32[2048]{0:T(1024)S(1)}, f32[2048]{0:T(1024)S(1)}, f32[2048]{0:T(1024)S(1)}, /*index=5*/f32[2048]{0:T(1024)S(1)}) fusion(f32[2048]{0:T(1024)S(1)} %bitcast.257, f32[1024]{0:T(1024)S(1)} %bitcast.269, f32[2048]{0:T(1024)S(1)} %bitcast.254, f32[1024]{0:T(1024)S(1)} %bitcast.272, ...), kind=kLoop, calls=%fused_computation.45.clone.1 | loop fusion | flops 85970944 | bytes 122880 | tf_op jit(solution)/shard_map/while/body/eval_jaxpr/reduce_sum | solution.py:29
  94.8 16.2 %fusion.64 = (f32[2048]{0:T(1024)S(1)}, f32[2048]{0:T(1024)S(1)}, f32[2048]{0:T(1024)S(1)}, f32[2048]{0:T(1024)S(1)}, f32[2048]{0:T(1024)S(1)}, /*index=5*/f32[2048]{0:T(1024)S(1)}) fusion(f32[2048]{0:T(1024)S(1)} %bitcast.257, f32[1024]{0:T(1024)S(1)} %bitcast.269, f32[2048]{0:T(1024)S(1)} %bitcast.254, f32[1024]{0:T(1024)S(1)} %bitcast.272, ...), kind=kLoop, calls=%fused_computation.45.clone.1 | loop fusion | flops 85970944 | bytes 122880 | tf_op jit(solution)/shard_map/while/body/eval_jaxpr/reduce_sum | solution.py:29
  111.2 16.2 %fusion.64 = (f32[2048]{0:T(1024)S(1)}, f32[2048]{0:T(1024)S(1)}, f32[2048]{0:T(1024)S(1)}, f32[2048]{0:T(1024)S(1)}, f32[2048]{0:T(1024)S(1)}, /*index=5*/f32[2048]{0:T(1024)S(1)}) fusion(f32[2048]{0:T(1024)S(1)} %bitcast.257, f32[1024]{0:T(1024)S(1)} %bitcast.269, f32[2048]{0:T(1024)S(1)} %bitcast.254, f32[1024]{0:T(1024)S(1)} %bitcast.272, ...), kind=kLoop, calls=%fused_computation.45.clone.1 | loop fusion | flops 85970944 | bytes 122880 | tf_op jit(solution)/shard_map/while/body/eval_jaxpr/reduce_sum | solution.py:29
  127.7 16.2 %fusion.64 = (f32[2048]{0:T(1024)S(1)}, f32[2048]{0:T(1024)S(1)}, f32[2048]{0:T(1024)S(1)}, f32[2048]{0:T(1024)S(1)}, f32[2048]{0:T(1024)S(1)}, /*index=5*/f32[2048]{0:T(1024)S(1)}) fusion(f32[2048]{0:T(1024)S(1)} %bitcast.257, f32[1024]{0:T(1024)S(1)} %bitcast.269, f32[2048]{0:T(1024)S(1)} %bitcast.254, f32[1024]{0:T(1024)S(1)} %bitcast.272, ...), kind=kLoop, calls=%fused_computation.45.clone.1 | loop fusion | flops 85970944 | bytes 122880 | tf_op jit(solution)/shard_map/while/body/eval_jaxpr/reduce_sum | solution.py:29
  144.1 16.2 %fusion.64 = (f32[2048]{0:T(1024)S(1)}, f32[2048]{0:T(1024)S(1)}, f32[2048]{0:T(1024)S(1)}, f32[2048]{0:T(1024)S(1)}, f32[2048]{0:T(1024)S(1)}, /*index=5*/f32[2048]{0:T(1024)S(1)}) fusion(f32[2048]{0:T(1024)S(1)} %bitcast.257, f32[1024]{0:T(1024)S(1)} %bitcast.269, f32[2048]{0:T(1024)S(1)} %bitcast.254, f32[1024]{0:T(1024)S(1)} %bitcast.272, ...), kind=kLoop, calls=%fused_computation.45.clone.1 | loop fusion | flops 85970944 | bytes 122880 | tf_op jit(solution)/shard_map/while/body/eval_jaxpr/reduce_sum | solution.py:29
  160.6 16.2 %fusion.64 = (f32[2048]{0:T(1024)S(1)}, f32[2048]{0:T(1024)S(1)}, f32[2048]{0:T(1024)S(1)}, f32[2048]{0:T(1024)S(1)}, f32[2048]{0:T(1024)S(1)}, /*index=5*/f32[2048]{0:T(1024)S(1)}) fusion(f32[2048]{0:T(1024)S(1)} %bitcast.257, f32[1024]{0:T(1024)S(1)} %bitcast.269, f32[2048]{0:T(1024)S(1)} %bitcast.254, f32[1024]{0:T(1024)S(1)} %bitcast.272, ...), kind=kLoop, calls=%fused_computation.45.clone.1 | loop fusion | flops 85970944 | bytes 122880 | tf_op jit(solution)/shard_map/while/body/eval_jaxpr/reduce_sum | solution.py:29
  177.1 16.2 %fusion.64 = (f32[2048]{0:T(1024)S(1)}, f32[2048]{0:T(1024)S(1)}, f32[2048]{0:T(1024)S(1)}, f32[2048]{0:T(1024)S(1)}, f32[2048]{0:T(1024)S(1)}, /*index=5*/f32[2048]{0:T(1024)S(1)}) fusion(f32[2048]{0:T(1024)S(1)} %bitcast.257, f32[1024]{0:T(1024)S(1)} %bitcast.269, f32[2048]{0:T(1024)S(1)} %bitcast.254, f32[1024]{0:T(1024)S(1)} %bitcast.272, ...), kind=kLoop, calls=%fused_computation.45.clone.1 | loop fusion | flops 85970944 | bytes 122880 | tf_op jit(solution)/shard_map/while/body/eval_jaxpr/reduce_sum | solution.py:29
  193.5 16.2 %fusion.64 = (f32[2048]{0:T(1024)S(1)}, f32[2048]{0:T(1024)S(1)}, f32[2048]{0:T(1024)S(1)}, f32[2048]{0:T(1024)S(1)}, f32[2048]{0:T(1024)S(1)}, /*index=5*/f32[2048]{0:T(1024)S(1)}) fusion(f32[2048]{0:T(1024)S(1)} %bitcast.257, f32[1024]{0:T(1024)S(1)} %bitcast.269, f32[2048]{0:T(1024)S(1)} %bitcast.254, f32[1024]{0:T(1024)S(1)} %bitcast.272, ...), kind=kLoop, calls=%fused_computation.45.clone.1 | loop fusion | flops 85970944 | bytes 122880 | tf_op jit(solution)/shard_map/while/body/eval_jaxpr/reduce_sum | solution.py:29
  210.0 16.2 %fusion.64 = (f32[2048]{0:T(1024)S(1)}, f32[2048]{0:T(1024)S(1)}, f32[2048]{0:T(1024)S(1)}, f32[2048]{0:T(1024)S(1)}, f32[2048]{0:T(1024)S(1)}, /*index=5*/f32[2048]{0:T(1024)S(1)}) fusion(f32[2048]{0:T(1024)S(1)} %bitcast.257, f32[1024]{0:T(1024)S(1)} %bitcast.269, f32[2048]{0:T(1024)S(1)} %bitcast.254, f32[1024]{0:T(1024)S(1)} %bitcast.272, ...), kind=kLoop, calls=%fused_computation.45.clone.1 | loop fusion | flops 85970944 | bytes 122880 | tf_op jit(solution)/shard_map/while/body/eval_jaxpr/reduce_sum | solution.py:29
  226.4 16.2 %fusion.64 = (f32[2048]{0:T(1024)S(1)}, f32[2048]{0:T(1024)S(1)}, f32[2048]{0:T(1024)S(1)}, f32[2048]{0:T(1024)S(1)}, f32[2048]{0:T(1024)S(1)}, /*index=5*/f32[2048]{0:T(1024)S(1)}) fusion(f32[2048]{0:T(1024)S(1)} %bitcast.257, f32[1024]{0:T(1024)S(1)} %bitcast.269, f32[2048]{0:T(1024)S(1)} %bitcast.254, f32[1024]{0:T(1024)S(1)} %bitcast.272, ...), kind=kLoop, calls=%fused_computation.45.clone.1 | loop fusion | flops 85970944 | bytes 122880 | tf_op jit(solution)/shard_map/while/body/eval_jaxpr/reduce_sum | solution.py:29
  242.9 16.2 %fusion.64 = (f32[2048]{0:T(1024)S(1)}, f32[2048]{0:T(1024)S(1)}, f32[2048]{0:T(1024)S(1)}, f32[2048]{0:T(1024)S(1)}, f32[2048]{0:T(1024)S(1)}, /*index=5*/f32[2048]{0:T(1024)S(1)}) fusion(f32[2048]{0:T(1024)S(1)} %bitcast.257, f32[1024]{0:T(1024)S(1)} %bitcast.269, f32[2048]{0:T(1024)S(1)} %bitcast.254, f32[1024]{0:T(1024)S(1)} %bitcast.272, ...), kind=kLoop, calls=%fused_computation.45.clone.1 | loop fusion | flops 85970944 | bytes 122880 | tf_op jit(solution)/shard_map/while/body/eval_jaxpr/reduce_sum | solution.py:29
  259.3 16.2 %fusion.64 = (f32[2048]{0:T(1024)S(1)}, f32[2048]{0:T(1024)S(1)}, f32[2048]{0:T(1024)S(1)}, f32[2048]{0:T(1024)S(1)}, f32[2048]{0:T(1024)S(1)}, /*index=5*/f32[2048]{0:T(1024)S(1)}) fusion(f32[2048]{0:T(1024)S(1)} %bitcast.257, f32[1024]{0:T(1024)S(1)} %bitcast.269, f32[2048]{0:T(1024)S(1)} %bitcast.254, f32[1024]{0:T(1024)S(1)} %bitcast.272, ...), kind=kLoop, calls=%fused_computation.45.clone.1 | loop fusion | flops 85970944 | bytes 122880 | tf_op jit(solution)/shard_map/while/body/eval_jaxpr/reduce_sum | solution.py:29
  275.8 16.2 %fusion.64 = (f32[2048]{0:T(1024)S(1)}, f32[2048]{0:T(1024)S(1)}, f32[2048]{0:T(1024)S(1)}, f32[2048]{0:T(1024)S(1)}, f32[2048]{0:T(1024)S(1)}, /*index=5*/f32[2048]{0:T(1024)S(1)}) fusion(f32[2048]{0:T(1024)S(1)} %bitcast.257, f32[1024]{0:T(1024)S(1)} %bitcast.269, f32[2048]{0:T(1024)S(1)} %bitcast.254, f32[1024]{0:T(1024)S(1)} %bitcast.272, ...), kind=kLoop, calls=%fused_computation.45.clone.1 | loop fusion | flops 85970944 | bytes 122880 | tf_op jit(solution)/shard_map/while/body/eval_jaxpr/reduce_sum | solution.py:29
  292.2 16.2 %fusion.64 = (f32[2048]{0:T(1024)S(1)}, f32[2048]{0:T(1024)S(1)}, f32[2048]{0:T(1024)S(1)}, f32[2048]{0:T(1024)S(1)}, f32[2048]{0:T(1024)S(1)}, /*index=5*/f32[2048]{0:T(1024)S(1)}) fusion(f32[2048]{0:T(1024)S(1)} %bitcast.257, f32[1024]{0:T(1024)S(1)} %bitcast.269, f32[2048]{0:T(1024)S(1)} %bitcast.254, f32[1024]{0:T(1024)S(1)} %bitcast.272, ...), kind=kLoop, calls=%fused_computation.45.clone.1 | loop fusion | flops 85970944 | bytes 122880 | tf_op jit(solution)/shard_map/while/body/eval_jaxpr/reduce_sum | solution.py:29
  308.7 16.2 %fusion.64 = (f32[2048]{0:T(1024)S(1)}, f32[2048]{0:T(1024)S(1)}, f32[2048]{0:T(1024)S(1)}, f32[2048]{0:T(1024)S(1)}, f32[2048]{0:T(1024)S(1)}, /*index=5*/f32[2048]{0:T(1024)S(1)}) fusion(f32[2048]{0:T(1024)S(1)} %bitcast.257, f32[1024]{0:T(1024)S(1)} %bitcast.269, f32[2048]{0:T(1024)S(1)} %bitcast.254, f32[1024]{0:T(1024)S(1)} %bitcast.272, ...), kind=kLoop, calls=%fused_computation.45.clone.1 | loop fusion | flops 85970944 | bytes 122880 | tf_op jit(solution)/shard_map/while/body/eval_jaxpr/reduce_sum | solution.py:29
  325.1 16.2 %fusion.64 = (f32[2048]{0:T(1024)S(1)}, f32[2048]{0:T(1024)S(1)}, f32[2048]{0:T(1024)S(1)}, f32[2048]{0:T(1024)S(1)}, f32[2048]{0:T(1024)S(1)}, /*index=5*/f32[2048]{0:T(1024)S(1)}) fusion(f32[2048]{0:T(1024)S(1)} %bitcast.257, f32[1024]{0:T(1024)S(1)} %bitcast.269, f32[2048]{0:T(1024)S(1)} %bitcast.254, f32[1024]{0:T(1024)S(1)} %bitcast.272, ...), kind=kLoop, calls=%fused_computation.45.clone.1 | loop fusion | flops 85970944 | bytes 122880 | tf_op jit(solution)/shard_map/while/body/eval_jaxpr/reduce_sum | solution.py:29
  348.2 1.4 scatter_fusion.1
  349.6 138.9 %all-reduce.3.cloned.1.call-done = f32[6,32768]{1,0:T(8,128)} async-done(((f32[6,32768]{1,0:T(8,128)}), f32[6,32768]{1,0:T(8,128)}) %all-reduce.3.cloned.1.call-update) | async-done | bytes 786448 | tf_op jit(solution)/shard_map/psum | solution.py:80
  489.6 1.4 scatter_fusion.2
  491.1 1.4 scatter_fusion.3
  492.6 1.4 scatter_fusion.4
  494.1 1.4 scatter_fusion
  498.0 64.6 %all-gather.3 = f32[128,6,256]{2,1,0:T(8,128)} all-gather(f32[1,6,256]{2,1,0:T(8,128)S(1)} %maximum_bitcast_fusion.1), channel_id=3, replica_groups=mesh['grp'=8,'dev'=16] {'grp','dev'}, dimensions={0}, use_global_device_ids=true | all-gather | bytes 792576 | tf_op jit(solution)/shard_map/all_gather | solution.py:77
  562.8 280.6 %while.21 = (s32[]{:T(128)}, f32[16,6,2048]{2,1,0:T(8,128)S(1)}, f32[3,1024]{1,0:T(4,128)S(1)}, f32[16,6,2048]{2,1,0:T(8,128)}, f32[3,1024]{1,0:T(4,128)S(1)}, /...) while((s32[]{:T(128)}, f32[16,6,2048]{2,1,0:T(8,128)S(1)}, ...), condition=%wide.region_21.22_spmd, body=%wide.region_14.21_spmd.sunk | while | flops 85970952 | bytes 499917 | solution.py:38
  564.0 16.2 %fusion.66 = (f32[2048]{0:T(1024)S(1)}, f32[2048]{0:T(1024)S(1)}, f32[2048]{0:T(1024)S(1)}, f32[2048]{0:T(1024)S(1)}, f32[2048]{0:T(1024)S(1)}, /*index=5*/f32[2048]{0:T(1024)S(1)}) fusion(f32[2048]{0:T(1024)S(1)} %bitcast.263, f32[1024]{0:T(1024)S(1)} %bitcast.275, f32[2048]{0:T(1024)S(1)} %bitcast.260, f32[1024]{0:T(1024)S(1)} %bitcast.278, ...), kind=kLoop, calls=%fused_computation.85.clone.1 | loop fusion | flops 85970944 | bytes 122880 | tf_op jit(solution)/shard_map/while/body/eval_jaxpr/reduce_sum | solution.py:29
  581.5 16.2 %fusion.66 = (f32[2048]{0:T(1024)S(1)}, f32[2048]{0:T(1024)S(1)}, f32[2048]{0:T(1024)S(1)}, f32[2048]{0:T(1024)S(1)}, f32[2048]{0:T(1024)S(1)}, /*index=5*/f32[2048]{0:T(1024)S(1)}) fusion(f32[2048]{0:T(1024)S(1)} %bitcast.263, f32[1024]{0:T(1024)S(1)} %bitcast.275, f32[2048]{0:T(1024)S(1)} %bitcast.260, f32[1024]{0:T(1024)S(1)} %bitcast.278, ...), kind=kLoop, calls=%fused_computation.85.clone.1 | loop fusion | flops 85970944 | bytes 122880 | tf_op jit(solution)/shard_map/while/body/eval_jaxpr/reduce_sum | solution.py:29
  599.2 16.2 %fusion.66 = (f32[2048]{0:T(1024)S(1)}, f32[2048]{0:T(1024)S(1)}, f32[2048]{0:T(1024)S(1)}, f32[2048]{0:T(1024)S(1)}, f32[2048]{0:T(1024)S(1)}, /*index=5*/f32[2048]{0:T(1024)S(1)}) fusion(f32[2048]{0:T(1024)S(1)} %bitcast.263, f32[1024]{0:T(1024)S(1)} %bitcast.275, f32[2048]{0:T(1024)S(1)} %bitcast.260, f32[1024]{0:T(1024)S(1)} %bitcast.278, ...), kind=kLoop, calls=%fused_computation.85.clone.1 | loop fusion | flops 85970944 | bytes 122880 | tf_op jit(solution)/shard_map/while/body/eval_jaxpr/reduce_sum | solution.py:29
  616.7 16.2 %fusion.66 = (f32[2048]{0:T(1024)S(1)}, f32[2048]{0:T(1024)S(1)}, f32[2048]{0:T(1024)S(1)}, f32[2048]{0:T(1024)S(1)}, f32[2048]{0:T(1024)S(1)}, /*index=5*/f32[2048]{0:T(1024)S(1)}) fusion(f32[2048]{0:T(1024)S(1)} %bitcast.263, f32[1024]{0:T(1024)S(1)} %bitcast.275, f32[2048]{0:T(1024)S(1)} %bitcast.260, f32[1024]{0:T(1024)S(1)} %bitcast.278, ...), kind=kLoop, calls=%fused_computation.85.clone.1 | loop fusion | flops 85970944 | bytes 122880 | tf_op jit(solution)/shard_map/while/body/eval_jaxpr/reduce_sum | solution.py:29
  634.2 16.2 %fusion.66 = (f32[2048]{0:T(1024)S(1)}, f32[2048]{0:T(1024)S(1)}, f32[2048]{0:T(1024)S(1)}, f32[2048]{0:T(1024)S(1)}, f32[2048]{0:T(1024)S(1)}, /*index=5*/f32[2048]{0:T(1024)S(1)}) fusion(f32[2048]{0:T(1024)S(1)} %bitcast.263, f32[1024]{0:T(1024)S(1)} %bitcast.275, f32[2048]{0:T(1024)S(1)} %bitcast.260, f32[1024]{0:T(1024)S(1)} %bitcast.278, ...), kind=kLoop, calls=%fused_computation.85.clone.1 | loop fusion | flops 85970944 | bytes 122880 | tf_op jit(solution)/shard_map/while/body/eval_jaxpr/reduce_sum | solution.py:29
  651.7 16.2 %fusion.66 = (f32[2048]{0:T(1024)S(1)}, f32[2048]{0:T(1024)S(1)}, f32[2048]{0:T(1024)S(1)}, f32[2048]{0:T(1024)S(1)}, f32[2048]{0:T(1024)S(1)}, /*index=5*/f32[2048]{0:T(1024)S(1)}) fusion(f32[2048]{0:T(1024)S(1)} %bitcast.263, f32[1024]{0:T(1024)S(1)} %bitcast.275, f32[2048]{0:T(1024)S(1)} %bitcast.260, f32[1024]{0:T(1024)S(1)} %bitcast.278, ...), kind=kLoop, calls=%fused_computation.85.clone.1 | loop fusion | flops 85970944 | bytes 122880 | tf_op jit(solution)/shard_map/while/body/eval_jaxpr/reduce_sum | solution.py:29
  669.3 16.2 %fusion.66 = (f32[2048]{0:T(1024)S(1)}, f32[2048]{0:T(1024)S(1)}, f32[2048]{0:T(1024)S(1)}, f32[2048]{0:T(1024)S(1)}, f32[2048]{0:T(1024)S(1)}, /*index=5*/f32[2048]{0:T(1024)S(1)}) fusion(f32[2048]{0:T(1024)S(1)} %bitcast.263, f32[1024]{0:T(1024)S(1)} %bitcast.275, f32[2048]{0:T(1024)S(1)} %bitcast.260, f32[1024]{0:T(1024)S(1)} %bitcast.278, ...), kind=kLoop, calls=%fused_computation.85.clone.1 | loop fusion | flops 85970944 | bytes 122880 | tf_op jit(solution)/shard_map/while/body/eval_jaxpr/reduce_sum | solution.py:29
  686.8 16.2 %fusion.66 = (f32[2048]{0:T(1024)S(1)}, f32[2048]{0:T(1024)S(1)}, f32[2048]{0:T(1024)S(1)}, f32[2048]{0:T(1024)S(1)}, f32[2048]{0:T(1024)S(1)}, /*index=5*/f32[2048]{0:T(1024)S(1)}) fusion(f32[2048]{0:T(1024)S(1)} %bitcast.263, f32[1024]{0:T(1024)S(1)} %bitcast.275, f32[2048]{0:T(1024)S(1)} %bitcast.260, f32[1024]{0:T(1024)S(1)} %bitcast.278, ...), kind=kLoop, calls=%fused_computation.85.clone.1 | loop fusion | flops 85970944 | bytes 122880 | tf_op jit(solution)/shard_map/while/body/eval_jaxpr/reduce_sum | solution.py:29
  704.3 16.2 %fusion.66 = (f32[2048]{0:T(1024)S(1)}, f32[2048]{0:T(1024)S(1)}, f32[2048]{0:T(1024)S(1)}, f32[2048]{0:T(1024)S(1)}, f32[2048]{0:T(1024)S(1)}, /*index=5*/f32[2048]{0:T(1024)S(1)}) fusion(f32[2048]{0:T(1024)S(1)} %bitcast.263, f32[1024]{0:T(1024)S(1)} %bitcast.275, f32[2048]{0:T(1024)S(1)} %bitcast.260, f32[1024]{0:T(1024)S(1)} %bitcast.278, ...), kind=kLoop, calls=%fused_computation.85.clone.1 | loop fusion | flops 85970944 | bytes 122880 | tf_op jit(solution)/shard_map/while/body/eval_jaxpr/reduce_sum | solution.py:29
  721.9 16.2 %fusion.66 = (f32[2048]{0:T(1024)S(1)}, f32[2048]{0:T(1024)S(1)}, f32[2048]{0:T(1024)S(1)}, f32[2048]{0:T(1024)S(1)}, f32[2048]{0:T(1024)S(1)}, /*index=5*/f32[2048]{0:T(1024)S(1)}) fusion(f32[2048]{0:T(1024)S(1)} %bitcast.263, f32[1024]{0:T(1024)S(1)} %bitcast.275, f32[2048]{0:T(1024)S(1)} %bitcast.260, f32[1024]{0:T(1024)S(1)} %bitcast.278, ...), kind=kLoop, calls=%fused_computation.85.clone.1 | loop fusion | flops 85970944 | bytes 122880 | tf_op jit(solution)/shard_map/while/body/eval_jaxpr/reduce_sum | solution.py:29
  739.4 16.2 %fusion.66 = (f32[2048]{0:T(1024)S(1)}, f32[2048]{0:T(1024)S(1)}, f32[2048]{0:T(1024)S(1)}, f32[2048]{0:T(1024)S(1)}, f32[2048]{0:T(1024)S(1)}, /*index=5*/f32[2048]{0:T(1024)S(1)}) fusion(f32[2048]{0:T(1024)S(1)} %bitcast.263, f32[1024]{0:T(1024)S(1)} %bitcast.275, f32[2048]{0:T(1024)S(1)} %bitcast.260, f32[1024]{0:T(1024)S(1)} %bitcast.278, ...), kind=kLoop, calls=%fused_computation.85.clone.1 | loop fusion | flops 85970944 | bytes 122880 | tf_op jit(solution)/shard_map/while/body/eval_jaxpr/reduce_sum | solution.py:29
  756.9 16.2 %fusion.66 = (f32[2048]{0:T(1024)S(1)}, f32[2048]{0:T(1024)S(1)}, f32[2048]{0:T(1024)S(1)}, f32[2048]{0:T(1024)S(1)}, f32[2048]{0:T(1024)S(1)}, /*index=5*/f32[2048]{0:T(1024)S(1)}) fusion(f32[2048]{0:T(1024)S(1)} %bitcast.263, f32[1024]{0:T(1024)S(1)} %bitcast.275, f32[2048]{0:T(1024)S(1)} %bitcast.260, f32[1024]{0:T(1024)S(1)} %bitcast.278, ...), kind=kLoop, calls=%fused_computation.85.clone.1 | loop fusion | flops 85970944 | bytes 122880 | tf_op jit(solution)/shard_map/while/body/eval_jaxpr/reduce_sum | solution.py:29
  774.5 16.2 %fusion.66 = (f32[2048]{0:T(1024)S(1)}, f32[2048]{0:T(1024)S(1)}, f32[2048]{0:T(1024)S(1)}, f32[2048]{0:T(1024)S(1)}, f32[2048]{0:T(1024)S(1)}, /*index=5*/f32[2048]{0:T(1024)S(1)}) fusion(f32[2048]{0:T(1024)S(1)} %bitcast.263, f32[1024]{0:T(1024)S(1)} %bitcast.275, f32[2048]{0:T(1024)S(1)} %bitcast.260, f32[1024]{0:T(1024)S(1)} %bitcast.278, ...), kind=kLoop, calls=%fused_computation.85.clone.1 | loop fusion | flops 85970944 | bytes 122880 | tf_op jit(solution)/shard_map/while/body/eval_jaxpr/reduce_sum | solution.py:29
  792.0 16.2 %fusion.66 = (f32[2048]{0:T(1024)S(1)}, f32[2048]{0:T(1024)S(1)}, f32[2048]{0:T(1024)S(1)}, f32[2048]{0:T(1024)S(1)}, f32[2048]{0:T(1024)S(1)}, /*index=5*/f32[2048]{0:T(1024)S(1)}) fusion(f32[2048]{0:T(1024)S(1)} %bitcast.263, f32[1024]{0:T(1024)S(1)} %bitcast.275, f32[2048]{0:T(1024)S(1)} %bitcast.260, f32[1024]{0:T(1024)S(1)} %bitcast.278, ...), kind=kLoop, calls=%fused_computation.85.clone.1 | loop fusion | flops 85970944 | bytes 122880 | tf_op jit(solution)/shard_map/while/body/eval_jaxpr/reduce_sum | solution.py:29
  809.5 16.2 %fusion.66 = (f32[2048]{0:T(1024)S(1)}, f32[2048]{0:T(1024)S(1)}, f32[2048]{0:T(1024)S(1)}, f32[2048]{0:T(1024)S(1)}, f32[2048]{0:T(1024)S(1)}, /*index=5*/f32[2048]{0:T(1024)S(1)}) fusion(f32[2048]{0:T(1024)S(1)} %bitcast.263, f32[1024]{0:T(1024)S(1)} %bitcast.275, f32[2048]{0:T(1024)S(1)} %bitcast.260, f32[1024]{0:T(1024)S(1)} %bitcast.278, ...), kind=kLoop, calls=%fused_computation.85.clone.1 | loop fusion | flops 85970944 | bytes 122880 | tf_op jit(solution)/shard_map/while/body/eval_jaxpr/reduce_sum | solution.py:29
  827.0 16.2 %fusion.66 = (f32[2048]{0:T(1024)S(1)}, f32[2048]{0:T(1024)S(1)}, f32[2048]{0:T(1024)S(1)}, f32[2048]{0:T(1024)S(1)}, f32[2048]{0:T(1024)S(1)}, /*index=5*/f32[2048]{0:T(1024)S(1)}) fusion(f32[2048]{0:T(1024)S(1)} %bitcast.263, f32[1024]{0:T(1024)S(1)} %bitcast.275, f32[2048]{0:T(1024)S(1)} %bitcast.260, f32[1024]{0:T(1024)S(1)} %bitcast.278, ...), kind=kLoop, calls=%fused_computation.85.clone.1 | loop fusion | flops 85970944 | bytes 122880 | tf_op jit(solution)/shard_map/while/body/eval_jaxpr/reduce_sum | solution.py:29
  849.1 141.8 %all-reduce.5.cloned.1.call-done = f32[6,32768]{1,0:T(8,128)} async-done(((f32[6,32768]{1,0:T(8,128)}), f32[6,32768]{1,0:T(8,128)}) %all-reduce.5.cloned.1.call-update) | async-done | bytes 786448 | tf_op jit(solution)/shard_map/psum | solution.py:80
  991.9 1.4 scatter_fusion.8
  994.2 1.4 scatter_fusion.7
  996.5 1.4 scatter_fusion.6
  998.8 1.4 scatter_fusion.5
  (207 shorter events, 49.1 us)
Async XLA Ops:
  7.2 481.4 %all-reduce.3.cloned.1.call-start = ((), (), s32[]{:S(2)}) async-start(), calls=%async_computation | async-start | bytes 2097152 | tf_op jit(solution)/shard_map/psum | solution.py:80
  341.5 1.0 copy-start.1
  341.5 1.1 copy-start.2
  341.5 1.3 copy-start.3
  341.5 1.6 copy-start.4
  342.5 0.8 copy-start.5
  342.6 648.3 %all-reduce.5.cloned.1.call-start = ((), (), s32[]{:S(2)}) async-start(), calls=%async_computation.1 | async-start | bytes 2097152 | tf_op jit(solution)/shard_map/psum | solution.py:80
  843.4 1.0 copy-start
Sparse Core Ops, SparseCore 0:
  342.7 145.8 all-reduce.2
  844.6 146.2 all-reduce.4
where the time goes:
time: 1010 us
  other arithmetic  525 us (52%)
  waiting for transfers between devices  281 us (28%)
  blocking collectives  129 us (13%)
  local copies, waits for them, and re-layouts  57.6 us (6%)
  between operations  14.4 us (1%)
    reduce_sum x32, other arithmetic, pair_block(): jnp.sum(weight * (drift_z - along * gap_z), axis=1)  519 us
    psum x2, waiting for transfers between devices, shards(): totals = lax.psum(terms, ('grp', 'dev'))  281 us
    all_gather x2, blocking collectives, shards(): gathered = lax.all_gather(targets[None], ('grp', 'dev'), axis=0, tiled=True)  129 us
  transfers between devices with their start and end apart: 2, of which 2 were waited for; matrix products, arithmetic and copies ran while one was open for 1% of the time, Pallas kernels for 0%

commit v1 on v0

--- a/solution.py
+++ b/solution.py
@@ -64,8 +64,11 @@
     star_dev = positions.shape[1]
     slot_cap = active_rows.shape[1]
     stars_all = star_dev * devices_all
+    live_all = stars_all // 8
     mass = 1.0 / stars_all
     soft_sq = 0.0004 * (131072.0 / stars_all) ** (2.0 / 3.0)
+    chunks = 4
+    chunk = live_all // chunks
     last_time = -(jnp.left_shift(jnp.int32(1), levels) - 1).astype(jnp.float32) * tick_length
     for step in range(active_rows.shape[0]):
         now = (step + 1) * tick_length
@@ -74,11 +77,28 @@
         targets = jnp.concatenate([pred_pos[:, rows], pred_vel[:, rows]], axis=0)
         step_counts = counts[step]
         own_count = step_counts[my_rank]
+        inclusive = jnp.cumsum(step_counts).astype(jnp.int32)
+        first = inclusive - step_counts
+        place = jnp.arange(live_all, dtype=jnp.int32)
+        owner = jnp.sum((inclusive[None, :] <= place[:, None]).astype(jnp.int32), axis=1)
+        owner = jnp.minimum(owner, devices_all - 1)
+        slot = owner * slot_cap + place - first[owner]
         gathered = lax.all_gather(targets[None], ("grp", "dev"), axis=0, tiled=True)
         flat = gathered.transpose(1, 0, 2).reshape(6, devices_all * slot_cap)
-        terms = block_terms(flat, pred_pos, pred_vel, mass, soft_sq)
-        totals = lax.psum(terms, ("grp", "dev"))
-        own = lax.dynamic_slice_in_dim(totals, my_rank * slot_cap, slot_cap, 1)
+        compact = flat[:, slot]
+        parts = []
+        summed = None
+        for c in range(chunks):
+            piece = compact[:, c * chunk:(c + 1) * chunk]
+            terms = block_terms(piece, pred_pos, pred_vel, mass, soft_sq)
+            if summed is not None:
+                terms, summed = lax.optimization_barrier((terms, summed))
+                parts.append(summed)
+            summed = lax.psum(terms, ("grp", "dev"))
+        parts.append(summed)
+        parts.append(jnp.zeros((6, slot_cap), jnp.float32))
+        totals = jnp.concatenate(parts, axis=1)
+        own = lax.dynamic_slice_in_dim(totals, first[my_rank], slot_cap, 1)
         span = now - last_time[rows]
         new_pos, new_vel = correct(
             positions[:, rows],

time: 1010 us -> 1740 us (1.72)
  waiting for transfers between devices: 281 us -> 913 us
  local copies, waits for them, and re-layouts: 57.6 us -> 405 us
  other arithmetic: 525 us -> 270 us
    psum x2 -> x8, waiting for transfers between devices: 281 us -> 913 us  [shards(): summed = lax.psum(terms, ('grp', 'dev'))]
    gather x0 -> x4, local copies, waits for them, and re-layouts: none -> 315 us  [the longest x2 194 us: shards(): slot = owner * slot_cap + place - first[owner]]
    reduce_sum x32 -> x16, other arithmetic: 519 us -> 259 us  [pair_block(): jnp.sum(weight * (drift_z - along * gap_z), axis=1)]
    slice x64 -> x32, local copies, waits for them, and re-layouts: 20.1 us -> 1.23 us  [pair_block(): drift_x = src_vel[0][None, :] - targets[3][:, None]]
  transfers between devices with their start and end apart: 2 -> 8, of which waited for: 2 -> 7; matrix products, arithmetic and copies ran while one was open for 1% -> 17% of each run, Pallas kernels for 0% -> 0%
where the time goes in v1:
time: 1740 us; the launch traced here: 1730 us
  waiting for transfers between devices  913 us (52%)
  local copies, waits for them, and re-layouts  405 us (23%)
  other arithmetic  270 us (16%)
  blocking collectives  123 us (7%)
  between operations  19.3 us (1%)
    psum x8, waiting for transfers between devices, shards(): summed = lax.psum(terms, ('grp', 'dev'))  913 us
    reduce_sum x16, other arithmetic, pair_block(): jnp.sum(weight * (drift_z - along * gap_z), axis=1)  259 us
    gather x2, local copies, waits for them, and re-layouts, shards(): slot = owner * slot_cap + place - first[owner]  194 us
    all_gather x2, blocking collectives, shards(): gathered = lax.all_gather(targets[None], ('grp', 'dev'), axis=0, tiled=True)  123 us
    gather x2, local copies, waits for them, and re-layouts, shards(): compact = flat[:, slot]  120 us
  transfers between devices with their start and end apart: 8, of which 7 were waited for; matrix products, arithmetic and copies ran while one was open for 17% of the time, Pallas kernels for 0%

profile of v1, /device:TPU:1, one launch (start us, length us, event | category | flops | bytes accessed | tf_op | source)
XLA Modules:
  0.0 1731.7 jit_solution(9103468403013295511)
XLA Ops:
  8.6 2.6 compare_select_fusion.4
  14.8 63.9 %all-gather.2 = f32[128,6,256]{2,1,0:T(8,128)S(1)} all-gather(f32[1,6,256]{2,1,0:T(8,128)S(1)} %maximum_bitcast_fusion), channel_id=2, replica_groups=mesh['grp'=8,'dev'=16] {'grp','dev'}, dimensions={0}, use_global_device_ids=true | all-gather | bytes 792576 | tf_op jit(solution)/shard_map/all_gather | solution.py:86
  78.7 8.4 copy.253
  87.8 2.3 convert_reduce_fusion.1
  90.3 97.2 %gather_fusion.6 = s32[16384]{0:T(1024)S(1)} fusion(s32[128]{0:T(128)S(1)} %get-tuple-element.734, s32[16384]{0:T(1024)S(1)} %broadcast_clamp_fusion.3), kind=kCustom, calls=%fused_computation.6 | custom fusion | bytes 196608 | tf_op jit(solution)/shard_map/gather | solution.py:85
  187.7 60.2 %gather_fusion.7 = f32[16384,6]{1,0:T(8,128)} fusion(f32[6,32768]{0,1:T(8,128)} %bitcast.632, s32[16384]{0:T(1024)S(1)} %broadcast_clamp_fusion.1), kind=kCustom, calls=%fused_computation.7 | custom fusion | bytes 851968 | tf_op jit(solution)/shard_map/gather | solution.py:88
  247.9 6.2 fusion.167
  256.3 32.8 %while.81 = (s32[]{:T(128)}, f32[2,6,2048]{2,1,0:T(8,128)S(1)}, f32[3,1024]{1,0:T(4,128)S(1)}, f32[2,6,2048]{2,1,0:T(8,128)S(1)}, f32[3,1024]{1,0:T(4,128)S(1)},...) while((s32[]{:T(128)}, f32[2,6,2048]{2,1,0:T(8,128)S(1)}, ...), condition=%wide.region_17.18_spmd, body=%wide.region_10.17_spmd.sunk | while | flops 85970952 | bytes 499925 | solution.py:38
  256.4 16.2 fusion.187
  272.8 16.2 fusion.187
  290.0 2.3 convert_reduce_fusion
  292.3 2.2 copy.255
  294.6 32.8 %while.80 = (s32[]{:T(128)}, f32[2,6,2048]{2,1,0:T(8,128)S(1)}, f32[3,1024]{1,0:T(4,128)S(1)}, f32[2,6,2048]{2,1,0:T(8,128)S(1)}, f32[3,1024]{1,0:T(4,128)S(1)},...) while((s32[]{:T(128)}, f32[2,6,2048]{2,1,0:T(8,128)S(1)}, ...), condition=%wide.region_9.10_spmd, body=%wide.region_2.9_spmd.sunk | while | flops 85970952 | bytes 499925 | solution.py:38
  294.7 16.2 fusion.185
  311.1 16.2 fusion.185
  327.4 2.3 copy.257
  329.7 32.8 %while.82 = (s32[]{:T(128)}, f32[2,6,2048]{2,1,0:T(8,128)S(1)}, f32[3,1024]{1,0:T(4,128)S(1)}, f32[2,6,2048]{2,1,0:T(8,128)S(1)}, f32[3,1024]{1,0:T(4,128)S(1)},...) while((s32[]{:T(128)}, f32[2,6,2048]{2,1,0:T(8,128)S(1)}, ...), condition=%wide.region_26.27_spmd, body=%wide.region_19.26_spmd.sunk | while | flops 85970952 | bytes 499925 | solution.py:38
  329.8 16.2 fusion.189
  346.2 16.2 fusion.189
  363.2 32.9 %while.83 = (s32[]{:T(128)}, f32[2,6,2048]{2,1,0:T(8,128)S(1)}, f32[3,1024]{1,0:T(4,128)S(1)}, f32[2,6,2048]{2,1,0:T(8,128)S(1)}, f32[3,1024]{1,0:T(4,128)S(1)},...) while((s32[]{:T(128)}, f32[2,6,2048]{2,1,0:T(8,128)S(1)}, ...), condition=%wide.region_35.36_spmd, body=%wide.region_28.35_spmd.sunk | while | flops 85970952 | bytes 499925 | solution.py:38
  363.3 16.2 fusion.191
  379.8 16.2 fusion.191
  399.3 97.2 %gather_fusion.15 = s32[16384]{0:T(1024)S(1)} fusion(s32[128]{0:T(128)S(1)} %get-tuple-element.733, s32[16384]{0:T(1024)S(1)} %broadcast_clamp_fusion.2), kind=kCustom, calls=%fused_computation.15 | custom fusion | bytes 196608 | tf_op jit(solution)/shard_map/gather | solution.py:85
  508.9 137.8 %all-reduce.11.cloned.1.call-done = f32[6,4096]{1,0:T(8,128)} async-done(((f32[6,4096]{1,0:T(8,128)}), f32[6,4096]{1,0:T(8,128)}) %all-reduce.11.cloned.1.call-update) | async-done | bytes 98320 | tf_op jit(solution)/shard_map/psum | solution.py:97
  647.7 141.3 %all-reduce.13.cloned.1.call-done = f32[6,4096]{1,0:T(8,128)} async-done(((f32[6,4096]{1,0:T(8,128)}), f32[6,4096]{1,0:T(8,128)}) %all-reduce.13.cloned.1.call-update) | async-done | bytes 98320 | tf_op jit(solution)/shard_map/psum | solution.py:97
  790.0 141.8 %all-reduce.15.cloned.1.call-done = f32[6,4096]{1,0:T(8,128)} async-done(((f32[6,4096]{1,0:T(8,128)}), f32[6,4096]{1,0:T(8,128)}) %all-reduce.15.cloned.1.call-update) | async-done | bytes 98320 | tf_op jit(solution)/shard_map/psum | solution.py:97
  941.4 59.1 %all-gather.3 = f32[128,6,256]{2,1,0:T(8,128)S(1)} all-gather(f32[1,6,256]{2,1,0:T(8,128)S(1)} %maximum_bitcast_fusion.1), channel_id=3, replica_groups=mesh['grp'=8,'dev'=16] {'grp','dev'}, dimensions={0}, use_global_device_ids=true | all-gather | bytes 792576 | tf_op jit(solution)/shard_map/all_gather | solution.py:86
  1000.5 8.4 copy.274
  1008.9 60.2 %gather_fusion.16 = f32[16384,6]{1,0:T(8,128)} fusion(f32[6,32768]{0,1:T(8,128)} %bitcast.633, s32[16384]{0:T(1024)S(1)} %broadcast_clamp_fusion), kind=kCustom, calls=%fused_computation.16 | custom fusion | bytes 851968 | tf_op jit(solution)/shard_map/gather | solution.py:88
  1069.1 6.2 fusion.166
  1077.5 32.8 %while.84 = (s32[]{:T(128)}, f32[2,6,2048]{2,1,0:T(8,128)S(1)}, f32[3,1024]{1,0:T(4,128)S(1)}, f32[2,6,2048]{2,1,0:T(8,128)S(1)}, f32[3,1024]{1,0:T(4,128)S(1)},...) while((s32[]{:T(128)}, f32[2,6,2048]{2,1,0:T(8,128)S(1)}, ...), condition=%wide.region_52.53_spmd, body=%wide.region_45.52_spmd.sunk | while | flops 85970952 | bytes 499925 | solution.py:38
  1077.6 16.2 fusion.193
  1094.0 16.2 fusion.193
  1110.3 2.3 copy.279
  1113.3 34.0 %while.85 = (s32[]{:T(128)}, f32[2,6,2048]{2,1,0:T(8,128)}, f32[3,1024]{1,0:T(4,128)S(1)}, f32[2,6,2048]{2,1,0:T(8,128)S(1)}, f32[3,1024]{1,0:T(4,128)S(1)}, /*i...) while((s32[]{:T(128)}, f32[2,6,2048]{2,1,0:T(8,128)}, f32[3,1024]{1,0:T(4,128)S(1)}, ...), condition=%wide.region_60.61_spmd, body=%wide.region_53.60_spmd.sunk | while | flops 85970952 | bytes 483541 | solution.py:38
  1113.4 16.2 fusion.195
  1130.3 16.2 fusion.195
  1147.6 2.2 copy.282
  1149.9 32.8 %while.86 = (s32[]{:T(128)}, f32[2,6,2048]{2,1,0:T(8,128)S(1)}, f32[3,1024]{1,0:T(4,128)S(1)}, f32[2,6,2048]{2,1,0:T(8,128)S(1)}, f32[3,1024]{1,0:T(4,128)S(1)},...) while((s32[]{:T(128)}, f32[2,6,2048]{2,1,0:T(8,128)S(1)}, ...), condition=%wide.region_69.70_spmd, body=%wide.region_62.69_spmd.sunk | while | flops 85970952 | bytes 499925 | solution.py:38
  1150.0 16.2 fusion.197
  1166.4 16.2 fusion.197
  1183.4 32.8 %while.87 = (s32[]{:T(128)}, f32[2,6,2048]{2,1,0:T(8,128)S(1)}, f32[3,1024]{1,0:T(4,128)S(1)}, f32[2,6,2048]{2,1,0:T(8,128)S(1)}, f32[3,1024]{1,0:T(4,128)S(1)},...) while((s32[]{:T(128)}, f32[2,6,2048]{2,1,0:T(8,128)S(1)}, ...), condition=%wide.region_78.79_spmd, body=%wide.region_71.78_spmd.sunk | while | flops 85970952 | bytes 499925 | solution.py:38
  1183.5 16.2 fusion.199
  1199.9 16.2 fusion.199
  1219.5 66.7 %all-reduce.17.cloned.1.call-done = f32[6,4096]{1,0:T(8,128)} async-done(((f32[6,4096]{1,0:T(8,128)}), f32[6,4096]{1,0:T(8,128)}) %all-reduce.17.cloned.1.call-update) | async-done | bytes 98320 | tf_op jit(solution)/shard_map/psum | solution.py:97
  1287.1 141.8 %all-reduce.19.cloned.1.call-done = f32[6,4096]{1,0:T(8,128)} async-done(((f32[6,4096]{1,0:T(8,128)}), f32[6,4096]{1,0:T(8,128)}) %all-reduce.19.cloned.1.call-update) | async-done | bytes 98320 | tf_op jit(solution)/shard_map/psum | solution.py:97
  1429.9 141.2 %all-reduce.21.cloned.1.call-done = f32[6,4096]{1,0:T(8,128)} async-done(((f32[6,4096]{1,0:T(8,128)}), f32[6,4096]{1,0:T(8,128)}) %all-reduce.21.cloned.1.call-update) | async-done | bytes 98320 | tf_op jit(solution)/shard_map/psum | solution.py:97
  1572.1 142.0 %all-reduce.23.cloned.1.call-done = f32[6,4096]{1,0:T(8,128)} async-done(((f32[6,4096]{1,0:T(8,128)}), f32[6,4096]{1,0:T(8,128)}) %all-reduce.23.cloned.1.call-update) | async-done | bytes 98320 | tf_op jit(solution)/shard_map/psum | solution.py:97
  (234 shorter events, 57.1 us)
Async XLA Ops:
  7.2 500.8 %all-reduce.9.cloned.1.call-start = ((), (), s32[]{:S(2)}) async-start(), calls=%async_computation | async-start | bytes 262144 | tf_op jit(solution)/shard_map/psum | solution.py:97
  78.7 11.5 copy-start.18
  289.1 0.6 copy-start.5
  289.8 356.9 %all-reduce.11.cloned.1.call-start = ((), (), s32[]{:S(2)}) async-start(), calls=%async_computation.1 | async-start | bytes 262144 | tf_op jit(solution)/shard_map/psum | solution.py:97
  327.4 2.3 copy-start.6
  362.6 0.7 copy-start.7
  396.1 100.5 %copy-start.8 = (f32[2,6,2048]{2,1,0:T(8,128)}, f32[2,6,2048]{2,1,0:T(8,128)S(1)}, u32[]{:S(2)}) copy-start(f32[2,6,2048]{2,1,0:T(8,128)S(1)} %get-tuple-element.238) | copy-start | bytes 294916
  397.5 542.8 %copy-start.15 = (s32[1024]{0:T(1024)}, s32[1024]{0:T(1024)S(1)}, u32[]{:S(2)}) copy-start(s32[1024]{0:T(1024)S(1)} %pad_clamp_fusion) | copy-start | bytes 12292
  399.3 99.4 %copy-start.11 = (f32[3,1024]{1,0:T(4,128)S(1)}, f32[3,1024]{1,0:T(4,128)}, u32[]{:S(2)}) copy-start(f32[3,1024]{1,0:T(4,128)} %param.23) | copy-start | bytes 36868
  399.3 99.6 %copy-start.12 = (f32[3,1024]{1,0:T(4,128)S(1)}, f32[3,1024]{1,0:T(4,128)}, u32[]{:S(2)}) copy-start(f32[3,1024]{1,0:T(4,128)} %param.25) | copy-start | bytes 36868
  399.3 99.8 %copy-start.13 = (f32[3,1024]{1,0:T(4,128)S(1)}, f32[3,1024]{1,0:T(4,128)}, u32[]{:S(2)}) copy-start(f32[3,1024]{1,0:T(4,128)} %param.24) | copy-start | bytes 36868
  399.3 100.7 %copy-start.14 = (f32[3,1024]{1,0:T(4,128)S(1)}, f32[3,1024]{1,0:T(4,128)}, u32[]{:S(2)}) copy-start(f32[3,1024]{1,0:T(4,128)} %param.26) | copy-start | bytes 36868
  507.9 281.0 %all-reduce.13.cloned.1.call-start = ((), (), s32[]{:S(2)}) async-start(), calls=%async_computation.2 | async-start | bytes 262144 | tf_op jit(solution)/shard_map/psum | solution.py:97
  646.7 285.0 %all-reduce.15.cloned.1.call-start = ((), (), s32[]{:S(2)}) async-start(), calls=%async_computation.3 | async-start | bytes 262144 | tf_op jit(solution)/shard_map/psum | solution.py:97
  789.0 497.1 %all-reduce.17.cloned.1.call-start = ((), (), s32[]{:S(2)}) async-start(), calls=%async_computation.4 | async-start | bytes 262144 | tf_op jit(solution)/shard_map/psum | solution.py:97
  934.3 74.6 %copy-start.2 = (f32[3,1024]{0,1:T(8,128)}, f32[3,1024]{0,1:T(8,128)S(1)}, u32[]{:S(2)}) copy-start(f32[3,1024]{0,1:T(8,128)S(1)} %scatter_fusion) | copy-start | bytes 36868
  935.8 73.1 %copy-start = (f32[3,1024]{0,1:T(8,128)}, f32[3,1024]{0,1:T(8,128)S(1)}, u32[]{:S(2)}) copy-start(f32[3,1024]{0,1:T(8,128)S(1)} %scatter_fusion.3) | copy-start | bytes 36868
  1110.3 2.9 copy-start.9
  1147.3 281.7 %all-reduce.19.cloned.1.call-start = ((), (), s32[]{:S(2)}) async-start(), calls=%async_computation.5 | async-start | bytes 262144 | tf_op jit(solution)/shard_map/psum | solution.py:97
  1182.7 0.7 copy-start.10
  1183.3 32.9 %copy-start.1 = (f32[3,1024]{0,1:T(8,128)S(1)}, f32[3,1024]{0,1:T(8,128)}, u32[]{:S(2)}) copy-start(f32[3,1024]{0,1:T(8,128)} %copy-done) | copy-start | bytes 36868
  1183.3 32.9 %copy-start.16 = (s32[1024]{0:T(1024)S(1)}, s32[1024]{0:T(1024)}, u32[]{:S(2)}) copy-start(s32[1024]{0:T(1024)} %copy-done.15) | copy-start | bytes 12292
  1183.4 34.3 %copy-start.3 = (f32[3,1024]{0,1:T(8,128)S(1)}, f32[3,1024]{0,1:T(8,128)}, u32[]{:S(2)}) copy-start(f32[3,1024]{0,1:T(8,128)} %copy-done.2) | copy-start | bytes 36868
  1183.4 531.6 %copy-start.19 = (f32[256]{0:T(256)S(1)}, f32[256]{0:T(256)}, u32[]{:S(2)}) copy-start(f32[256]{0:T(256)} %get-tuple-element.731) | copy-start | bytes 3076
  1183.4 531.6 %copy-start.20 = (f32[256]{0:T(256)S(1)}, f32[256]{0:T(256)}, u32[]{:S(2)}) copy-start(f32[256]{0:T(256)} %get-tuple-element.732) | copy-start | bytes 3076
  1183.4 531.9 %copy-start.17 = (s32[256,1]{0,1:T(1,128)S(1)}, s32[256,1]{0,1:T(1,128)}, u32[]{:S(2)}) copy-start(s32[256,1]{0,1:T(1,128)} %get-tuple-element.729) | copy-start | bytes 3076
  1216.2 355.0 %copy-start.4 = (f32[2,6,2048]{2,1,0:T(8,128)}, f32[2,6,2048]{2,1,0:T(8,128)S(1)}, u32[]{:S(2)}) copy-start(f32[2,6,2048]{2,1,0:T(8,128)S(1)} %get-tuple-element.248) | copy-start | bytes 294916
  1286.2 285.0 %all-reduce.21.cloned.1.call-start = ((), (), s32[]{:S(2)}) async-start(), calls=%async_computation.6 | async-start | bytes 262144 | tf_op jit(solution)/shard_map/psum | solution.py:97
  1429.0 285.1 %all-reduce.23.cloned.1.call-start = ((), (), s32[]{:S(2)}) async-start(), calls=%async_computation.7 | async-start | bytes 262144 | tf_op jit(solution)/shard_map/psum | solution.py:97
Sparse Core Ops, SparseCore 0:
  289.9 138.6 all-reduce.8
  508.1 138.5 all-reduce.10
  651.4 137.4 all-reduce.12
  794.3 137.4 all-reduce.14
  1147.4 138.6 all-reduce.16
  1291.4 137.4 all-reduce.18
  1433.7 137.4 all-reduce.20
  1576.6 137.4 all-reduce.22
